TPU v7x, 32 devices: a whole 2x2x4 slice. The times are simulated.
32 devices in a mesh: rep: 4 (over y, core), fsdp: 4 (over z), seq: 2 (over x).
Axes of the slice: x: 2, y: 2, z: 4, core: 2. Of those that a mesh axis runs over, the one named last changes fastest.
Arguments:
- tokens: bfloat16 [16, 1024, 1024], P(('rep', 'fsdp'), 'seq'), may hold values from -6 to 6
- positions: int32 [3, 16, 1024], P(None, ('rep', 'fsdp'), 'seq'), may hold values from 0 to 15
- input_gain: bfloat16 [1024], P('fsdp'), may hold values from 0.5 to 1.5
- input_shift: bfloat16 [1024], P('fsdp'), may hold values from -1.5 to 1.5
- joint_weight: bfloat16 [1024, 3072], P('fsdp'), may hold values from -0.1875 to 0.1875
- joint_bias: bfloat16 [3072], P('fsdp'), may hold values from -1.5 to 1.5
- output_weight: bfloat16 [1024, 1024], P('fsdp'), may hold values from -3 to 3
- output_bias: bfloat16 [1024], P('fsdp'), may hold values from -1.5 to 1.5
- middle_gain: bfloat16 [1024], P('fsdp'), may hold values from 0.5 to 1.5
- middle_shift: bfloat16 [1024], P('fsdp'), may hold values from -1.5 to 1.5
- expand_weight: bfloat16 [1024, 4096], P('fsdp'), may hold values from -0.1875 to 0.1875
- expand_bias: bfloat16 [4096], P('fsdp'), may hold values from -2.5 to 2.5
- reduce_weight: bfloat16 [4096, 1024], P('fsdp'), may hold values from -0.09375 to 0.09375
- reduce_bias: bfloat16 [1024], P('fsdp'), may hold values from -1.5 to 1.5
- cotangent: bfloat16 [16, 1024, 1024], P(('rep', 'fsdp'), 'seq'), may hold values from -6 to 6
Outputs:
- block_output: bfloat16 [16, 1024, 1024], P(('rep', 'fsdp'), 'seq')
- input_gradient: float32 [16, 1024, 1024], P(('rep', 'fsdp'), 'seq')
- input_gain_gradient: float32 [1024], P('fsdp')
- input_shift_gradient: float32 [1024], P('fsdp')
- joint_weight_gradient: float32 [1024, 3072], P('fsdp')
- joint_bias_gradient: float32 [3072], P('fsdp')
- output_weight_gradient: float32 [1024, 1024], P('fsdp')
- output_bias_gradient: float32 [1024], P('fsdp')
- middle_gain_gradient: float32 [1024], P('fsdp')
- middle_shift_gradient: float32 [1024], P('fsdp')
- expand_weight_gradient: float32 [1024, 4096], P('fsdp')
- expand_bias_gradient: float32 [4096], P('fsdp')
- reduce_weight_gradient: float32 [4096, 1024], P('fsdp')
- reduce_bias_gradient: float32 [1024], P('fsdp')
All inputs are finite; a program needn't handle non-finite values.
Results may differ from a plain program's by a relative error of at most 0.018.
Values may be sent and summed in bfloat16 or wider, within the bound.
No kernel may reach another device: no remote copies, remote signals or barrier semaphores. Data moves between devices by JAX's collectives and lax.ppermute only.
A program may use at most 192 MiB of HBM per device.

v0:
```python
import jax
import jax.numpy as jnp
from jax import lax
from jax.sharding import PartitionSpec as P

epsilon = 1e-06


def norm_rows(values, gains, shifts):
    average = jnp.mean(values, axis=-1, keepdims=True)
    centred = values - average
    spread = jnp.mean(centred * centred, axis=-1, keepdims=True)
    return centred * lax.rsqrt(spread + epsilon) * gains + shifts


def rotary_tables(positions):
    counter = jnp.arange(10).astype(jnp.float32)
    frequency = jnp.power(10000.0, -counter / 10.0)
    angles = positions.astype(jnp.float32)[:, :, None] * frequency
    angles = jnp.transpose(angles, (1, 0, 2))
    return (jnp.cos(angles), jnp.sin(angles))


def rotate(values, cosine_part, sine_part):
    length = values.shape[0]
    heads_count = values.shape[1]
    turned = values[:, :, :60].reshape(length, heads_count, 3, 2, 10)
    former = turned[:, :, :, 0, :]
    latter = turned[:, :, :, 1, :]
    cosine_wide = cosine_part[:, None, :, :]
    sine_wide = sine_part[:, None, :, :]
    new_former = former * cosine_wide - latter * sine_wide
    new_latter = latter * cosine_wide + former * sine_wide
    joined = jnp.stack([new_former, new_latter], axis=3).reshape(length, heads_count, 60)
    return jnp.concatenate([joined, values[:, :, 60:]], axis=2)


def exact_gelu(values):
    return jax.nn.gelu(values, approximate=False)


def split_heads(block):
    return block.reshape(block.shape[0], block.shape[1] // 64, 64)


def group_scores(query_heads, key_heads):
    return (
        jnp.einsum("thd,shd->hts", query_heads, key_heads, preferred_element_type=jnp.float32)
        * 0.125
    )


def attend(inputs):
    query_block, key_block, value_block = inputs
    query_heads = split_heads(query_block)
    key_heads = split_heads(key_block)
    value_heads = split_heads(value_block)
    scores = group_scores(query_heads, key_heads)
    row_max = jnp.max(scores, axis=2, keepdims=True)
    raised = jnp.exp(scores - row_max)
    row_total = jnp.sum(raised, axis=2, keepdims=True)
    probs_low = (raised / row_total).astype(jnp.bfloat16)
    mixed = jnp.einsum("hts,shd->thd", probs_low, value_heads, preferred_element_type=jnp.float32)
    return (mixed.reshape(query_block.shape[0], -1), row_max, row_total)


def attend_back(inputs):
    query_block, key_block, value_block, grad_block, row_max, row_total = inputs
    query_heads = split_heads(query_block)
    key_heads = split_heads(key_block)
    value_heads = split_heads(value_block)
    grad_heads = split_heads(grad_block)
    scores = group_scores(query_heads, key_heads)
    probs = jnp.exp(scores - row_max) / row_total
    probs_low = probs.astype(jnp.bfloat16)
    grad_probs = jnp.einsum(
        "thd,shd->hts", grad_heads, value_heads, preferred_element_type=jnp.float32
    )
    value_grad = jnp.einsum(
        "hts,thd->shd", probs_low, grad_heads, preferred_element_type=jnp.float32
    )
    inner = jnp.sum(grad_probs * probs, axis=2, keepdims=True)
    grad_scores = (probs * (grad_probs - inner)).astype(jnp.bfloat16)
    query_grad = (
        jnp.einsum("hts,shd->thd", grad_scores, key_heads, preferred_element_type=jnp.float32)
        * 0.125
    )
    key_grad = (
        jnp.einsum("hts,thd->shd", grad_scores, query_heads, preferred_element_type=jnp.float32)
        * 0.125
    )
    return (
        query_grad.reshape(query_block.shape[0], -1),
        key_grad.reshape(key_block.shape[0], -1),
        value_grad.reshape(key_block.shape[0], -1),
    )


def local(
    tokens,
    positions,
    input_gain,
    input_shift,
    joint_weight,
    joint_bias,
    output_weight,
    output_bias,
    middle_gain,
    middle_shift,
    expand_weight,
    expand_bias,
    reduce_weight,
    reduce_bias,
    cotangent,
):
    shards = (
        input_gain,
        input_shift,
        joint_weight,
        joint_bias,
        output_weight,
        output_bias,
        middle_gain,
        middle_shift,
        expand_weight,
        expand_bias,
        reduce_weight,
        reduce_bias,
    )
    gathered = (
        lax.all_gather(shards[0], "fsdp", axis=0, tiled=True),
        lax.all_gather(shards[1], "fsdp", axis=0, tiled=True),
        lax.all_gather(shards[2], "fsdp", axis=0, tiled=True),
        lax.all_gather(shards[3], "fsdp", axis=0, tiled=True),
        lax.all_gather(shards[4], "fsdp", axis=0, tiled=True),
        lax.all_gather(shards[5], "fsdp", axis=0, tiled=True),
        lax.all_gather(shards[6], "fsdp", axis=0, tiled=True),
        lax.all_gather(shards[7], "fsdp", axis=0, tiled=True),
        lax.all_gather(shards[8], "fsdp", axis=0, tiled=True),
        lax.all_gather(shards[9], "fsdp", axis=0, tiled=True),
        lax.all_gather(shards[10], "fsdp", axis=0, tiled=True),
        lax.all_gather(shards[11], "fsdp", axis=0, tiled=True),
    )
    row_count = tokens.shape[1]
    width = tokens.shape[2]
    head_count = width // 64
    per_group = min(4, head_count)
    group_count = head_count // per_group
    group_width = per_group * 64

    def to_groups(block):
        return jnp.transpose(block.reshape(block.shape[0], group_count, group_width), (1, 0, 2))

    def from_groups(block):
        return jnp.transpose(block, (1, 0, 2)).reshape(block.shape[1], width)

    residual_in = tokens[0].astype(jnp.float32)
    cosine_part, sine_part = rotary_tables(positions[:, 0, :])
    normed_in = norm_rows(
        residual_in, gathered[0].astype(jnp.float32), gathered[1].astype(jnp.float32)
    ).astype(jnp.bfloat16)
    projected = jnp.dot(normed_in, gathered[2], preferred_element_type=jnp.float32) + gathered[
        3
    ].astype(jnp.float32)
    queries = (
        rotate(projected[:, :width].reshape(row_count, head_count, 64), cosine_part, sine_part)
        .astype(jnp.bfloat16)
        .reshape(row_count, width)
    )
    keys = (
        rotate(
            projected[:, width : 2 * width].reshape(row_count, head_count, 64),
            cosine_part,
            sine_part,
        )
        .astype(jnp.bfloat16)
        .reshape(row_count, width)
    )
    values = projected[:, 2 * width :].astype(jnp.bfloat16)
    query_groups = to_groups(queries)
    key_all, value_all = (
        lax.all_gather(to_groups(keys), "seq", axis=1, tiled=True),
        lax.all_gather(to_groups(values), "seq", axis=1, tiled=True),
    )
    mixed, row_max, row_total = lax.map(attend, (query_groups, key_all, value_all))
    attended = from_groups(mixed).astype(jnp.bfloat16)
    residual_mid = residual_in + (
        jnp.dot(attended, gathered[4], preferred_element_type=jnp.float32)
        + gathered[5].astype(jnp.float32)
    )
    normed_mid = norm_rows(
        residual_mid, gathered[6].astype(jnp.float32), gathered[7].astype(jnp.float32)
    ).astype(jnp.bfloat16)
    upper = jnp.dot(normed_mid, gathered[8], preferred_element_type=jnp.float32) + gathered[
        9
    ].astype(jnp.float32)
    hidden = exact_gelu(upper).astype(jnp.bfloat16)
    result = residual_mid + (
        jnp.dot(hidden, gathered[10], preferred_element_type=jnp.float32)
        + gathered[11].astype(jnp.float32)
    )
    block_output = result.astype(jnp.bfloat16)[None]
    again = (
        lax.all_gather(shards[0], "fsdp", axis=0, tiled=True),
        lax.all_gather(shards[1], "fsdp", axis=0, tiled=True),
        lax.all_gather(shards[2], "fsdp", axis=0, tiled=True),
        lax.all_gather(shards[3], "fsdp", axis=0, tiled=True),
        lax.all_gather(shards[4], "fsdp", axis=0, tiled=True),
        lax.all_gather(shards[5], "fsdp", axis=0, tiled=True),
        lax.all_gather(shards[6], "fsdp", axis=0, tiled=True),
        lax.all_gather(shards[7], "fsdp", axis=0, tiled=True),
        lax.all_gather(shards[8], "fsdp", axis=0, tiled=True),
        lax.all_gather(shards[9], "fsdp", axis=0, tiled=True),
        lax.all_gather(shards[10], "fsdp", axis=0, tiled=True),
        lax.all_gather(shards[11], "fsdp", axis=0, tiled=True),
    )
    grad_low = cotangent[0]
    grad_out = grad_low.astype(jnp.float32)
    reduce_term = jnp.einsum("tf,td->fd", hidden, grad_low, preferred_element_type=jnp.float32)
    reduce_offset_term = jnp.sum(grad_out, axis=0)
    grad_hidden = jnp.einsum("td,fd->tf", grad_low, again[10], preferred_element_type=jnp.float32)
    gelu_pull = jax.vjp(exact_gelu, upper)[1]
    grad_upper = gelu_pull(grad_hidden)[0].astype(jnp.bfloat16)
    expand_term = jnp.einsum(
        "td,tf->df", normed_mid, grad_upper, preferred_element_type=jnp.float32
    )
    expand_offset_term = jnp.sum(grad_upper.astype(jnp.float32), axis=0)
    grad_mid_norm = jnp.einsum(
        "tf,df->td", grad_upper, again[8], preferred_element_type=jnp.float32
    )
    middle_pull = jax.vjp(
        norm_rows, residual_mid, again[6].astype(jnp.float32), again[7].astype(jnp.float32)
    )[1]
    grad_mid_in, middle_gain_term, middle_shift_term = middle_pull(grad_mid_norm)
    grad_resid = grad_out + grad_mid_in
    grad_branch = grad_resid.astype(jnp.bfloat16)
    output_term = jnp.einsum("td,te->de", attended, grad_branch, preferred_element_type=jnp.float32)
    output_offset_term = jnp.sum(grad_branch.astype(jnp.float32), axis=0)
    grad_attended = jnp.einsum(
        "te,de->td", grad_branch, again[4], preferred_element_type=jnp.float32
    ).astype(jnp.bfloat16)
    query_grad, key_grad, value_grad = lax.map(
        attend_back,
        (query_groups, key_all, value_all, to_groups(grad_attended), row_max, row_total),
    )
    key_share, value_share = (
        lax.psum_scatter(
            key_grad.astype(jnp.bfloat16), "seq", scatter_dimension=1, tiled=True
        ).astype(jnp.float32),
        lax.psum_scatter(
            value_grad.astype(jnp.bfloat16), "seq", scatter_dimension=1, tiled=True
        ).astype(jnp.float32),
    )
    grad_query = rotate(
        from_groups(query_grad).reshape(row_count, head_count, 64), cosine_part, -sine_part
    ).reshape(row_count, width)
    grad_key = rotate(
        from_groups(key_share).reshape(row_count, head_count, 64), cosine_part, -sine_part
    ).reshape(row_count, width)
    grad_value = from_groups(value_share)
    grad_projected = jnp.concatenate([grad_query, grad_key, grad_value], axis=1).astype(
        jnp.bfloat16
    )
    joint_term = jnp.einsum(
        "td,te->de", normed_in, grad_projected, preferred_element_type=jnp.float32
    )
    joint_offset_term = jnp.sum(grad_projected.astype(jnp.float32), axis=0)
    grad_in_norm = jnp.einsum(
        "te,de->td", grad_projected, again[2], preferred_element_type=jnp.float32
    )
    input_pull = jax.vjp(
        norm_rows, residual_in, again[0].astype(jnp.float32), again[1].astype(jnp.float32)
    )[1]
    grad_first_in, input_gain_term, input_shift_term = input_pull(grad_in_norm)
    input_gradient = (grad_resid + grad_first_in)[None]
    terms = (
        input_gain_term,
        input_shift_term,
        joint_term,
        joint_offset_term,
        output_term,
        output_offset_term,
        middle_gain_term,
        middle_shift_term,
        expand_term,
        expand_offset_term,
        reduce_term,
        reduce_offset_term,
    )
    owned = (
        lax.psum_scatter(
            terms[0].astype(jnp.bfloat16), "fsdp", scatter_dimension=0, tiled=True
        ).astype(jnp.float32),
        lax.psum_scatter(
            terms[1].astype(jnp.bfloat16), "fsdp", scatter_dimension=0, tiled=True
        ).astype(jnp.float32),
        lax.psum_scatter(
            terms[2].astype(jnp.bfloat16), "fsdp", scatter_dimension=0, tiled=True
        ).astype(jnp.float32),
        lax.psum_scatter(
            terms[3].astype(jnp.bfloat16), "fsdp", scatter_dimension=0, tiled=True
        ).astype(jnp.float32),
        lax.psum_scatter(
            terms[4].astype(jnp.bfloat16), "fsdp", scatter_dimension=0, tiled=True
        ).astype(jnp.float32),
        lax.psum_scatter(
            terms[5].astype(jnp.bfloat16), "fsdp", scatter_dimension=0, tiled=True
        ).astype(jnp.float32),
        lax.psum_scatter(
            terms[6].astype(jnp.bfloat16), "fsdp", scatter_dimension=0, tiled=True
        ).astype(jnp.float32),
        lax.psum_scatter(
            terms[7].astype(jnp.bfloat16), "fsdp", scatter_dimension=0, tiled=True
        ).astype(jnp.float32),
        lax.psum_scatter(
            terms[8].astype(jnp.bfloat16), "fsdp", scatter_dimension=0, tiled=True
        ).astype(jnp.float32),
        lax.psum_scatter(
            terms[9].astype(jnp.bfloat16), "fsdp", scatter_dimension=0, tiled=True
        ).astype(jnp.float32),
        lax.psum_scatter(
            terms[10].astype(jnp.bfloat16), "fsdp", scatter_dimension=0, tiled=True
        ).astype(jnp.float32),
        lax.psum_scatter(
            terms[11].astype(jnp.bfloat16), "fsdp", scatter_dimension=0, tiled=True
        ).astype(jnp.float32),
    )
    summed = (
        lax.psum(owned[0].astype(jnp.bfloat16), ("rep", "seq")).astype(jnp.float32),
        lax.psum(owned[1].astype(jnp.bfloat16), ("rep", "seq")).astype(jnp.float32),
        lax.psum(owned[2].astype(jnp.bfloat16), ("rep", "seq")).astype(jnp.float32),
        lax.psum(owned[3].astype(jnp.bfloat16), ("rep", "seq")).astype(jnp.float32),
        lax.psum(owned[4].astype(jnp.bfloat16), ("rep", "seq")).astype(jnp.float32),
        lax.psum(owned[5].astype(jnp.bfloat16), ("rep", "seq")).astype(jnp.float32),
        lax.psum(owned[6].astype(jnp.bfloat16), ("rep", "seq")).astype(jnp.float32),
        lax.psum(owned[7].astype(jnp.bfloat16), ("rep", "seq")).astype(jnp.float32),
        lax.psum(owned[8].astype(jnp.bfloat16), ("rep", "seq")).astype(jnp.float32),
        lax.psum(owned[9].astype(jnp.bfloat16), ("rep", "seq")).astype(jnp.float32),
        lax.psum(owned[10].astype(jnp.bfloat16), ("rep", "seq")).astype(jnp.float32),
        lax.psum(owned[11].astype(jnp.bfloat16), ("rep", "seq")).astype(jnp.float32),
    )
    return (
        block_output,
        input_gradient,
        summed[0],
        summed[1],
        summed[2],
        summed[3],
        summed[4],
        summed[5],
        summed[6],
        summed[7],
        summed[8],
        summed[9],
        summed[10],
        summed[11],
    )


def solution(mesh):
    return jax.shard_map(
        local,
        mesh=mesh,
        in_specs=(
            P(("rep", "fsdp"), "seq", None),
            P(None, ("rep", "fsdp"), "seq"),
            P("fsdp"),
            P("fsdp"),
            P("fsdp", None),
            P("fsdp"),
            P("fsdp", None),
            P("fsdp"),
            P("fsdp"),
            P("fsdp"),
            P("fsdp", None),
            P("fsdp"),
            P("fsdp", None),
            P("fsdp"),
            P(("rep", "fsdp"), "seq", None),
        ),
        out_specs=(
            P(("rep", "fsdp"), "seq", None),
            P(("rep", "fsdp"), "seq", None),
            P("fsdp"),
            P("fsdp"),
            P("fsdp", None),
            P("fsdp"),
            P("fsdp", None),
            P("fsdp"),
            P("fsdp"),
            P("fsdp"),
            P("fsdp", None),
            P("fsdp"),
            P("fsdp", None),
            P("fsdp"),
        ),
        check_vma=False,
    )
```

profile of v0, /device:TPU:0, one launch (start us, length us, event | category | flops | bytes accessed | tf_op | source)
XLA Modules:
  0.0 1273.0 jit_solution(16139119386478265900)
XLA Ops:
  8.6 14.8 %all-gather.2 = bf16[4,1,768]{2,1,0:T(2,128)(2,1)S(1)} all-gather(bf16[1,1,768]{2,1,0:T(2,128)(2,1)S(1)} %reshape.244), channel_id=1, replica_groups=mesh['rep'=4,'fsdp'=4,'seq'=2] {'fsdp'}, dimensions={0}, use_global_device_ids=true | all-gather | bytes 7680 | tf_op jit(solution)/shard_map/all_gather | solution.py:134
  24.2 12.4 all-gather.1
  49.0 78.8 %all-gather.14.cloned.1.call-done = bf16[1024,3072]{1,0:T(8,128)(2,1)} async-done(((bf16[256,3072]{1,0:T(8,128)(2,1)}), bf16[1024,3072]{1,0:T(8,128)(2,1)}) %all-gather.14.cloned.1.call-update) | async-done | bytes 6291472 | tf_op jit(solution)/shard_map/all_gather | solution.py:133
  167.4 11.9 all_gather.59
  187.7 9.1 all-gather.4
  204.7 31.5 %while.30 = (s32[]{:T(128)}, bf16[4,512,256]{1,2,0:T(8,128)(2,1)S(1)}, f32[4,4,512,1]{2,1,3,0:T(4,128)S(1)}, f32[4,4,512,1]{2,1,3,0:T(4,128)S(1)}, bf16[4,1024,2...) while((s32[]{:T(128)}, ...), condition=%wide.region_5.6_spmd.clone, body=%wide.region_2.5_spmd.sunk.clone | while | flops 555741184 | bytes 29958248 | solution.py:185
  236.2 15.6 %all-gather.20.cloned.1.call-done = bf16[1024,1024]{1,0:T(8,128)(2,1)} async-done(((bf16[256,1024]{1,0:T(8,128)(2,1)}), bf16[1024,1024]{1,0:T(8,128)(2,1)}) %all-gather.20.cloned.1.call-update) | async-done | bytes 2097168 | tf_op jit(solution)/shard_map/all_gather | solution.py:135
  255.5 146.2 %all-gather.22.cloned.1.call-done = bf16[1024,4096]{1,0:T(8,128)(2,1)} async-done(((bf16[256,4096]{1,0:T(8,128)(2,1)}), bf16[1024,4096]{1,0:T(8,128)(2,1)}) %all-gather.22.cloned.1.call-update) | async-done | bytes 8388624 | tf_op jit(solution)/shard_map/all_gather | solution.py:139
  401.7 27.6 %multiply_convert_fusion.1 = (bf16[512,4096]{1,0:T(8,128)(2,1)}, f32[512,4096]{1,0:T(8,128)}, f32[512,4096]{1,0:T(8,128)}) fusion(f32[4096]{0:T(1024)S(1)} %convert_element_type.220, bf16[1024,4096]{1,0:T(8,128)(2,1)} %all-gather.22.cloned.1.call-done, f32[512,1024]{1,0:T(8,128)S(1)} %get-tuple-element.210, f32[1024]{0:T(1024)S(1)} %bitcast.295, ...), kind=kOutput, calls=%fused_computation.31 | convolution fusion | flops 4436000768 | bytes 31485952 | tf_op jit(solution)/shard_map/dot_general | solution.py:194
  429.3 121.7 %all-gather.24.cloned.1.call-done = bf16[4096,1024]{1,0:T(8,128)(2,1)} async-done(((bf16[1024,1024]{1,0:T(8,128)(2,1)}), bf16[4096,1024]{1,0:T(8,128)(2,1)}) %all-gather.24.cloned.1.call-update) | async-done | bytes 8388624 | tf_op jit(solution)/shard_map/all_gather | solution.py:141
  550.9 15.9 %fusion.47 = (bf16[4096]{0:T(1024)(128)(2,1)}, bf16[512,4096]{1,0:T(8,128)(2,1)}) fusion(f32[512,4096]{1,0:T(8,128)} %get-tuple-element.179, bf16[4096,1024]{1,0:T(8,128)(2,1)} %all-gather.24.cloned.1.call-done, bf16[1,512,1024]{2,1,0:T(8,128)(2,1)S(1)} %copy-done.7, f32[512,4096]{1,0:T(8,128)} %get-tuple-element.211, f32[4096]{0:T(1024)S(1)} %convert_element_type.220), kind=kOutput, calls=%fused_computation.125 | convolution fusion | flops 4328517632 | bytes 30433280 | tf_op jit(solution)/shard_map/td,fd->tf/dot_general | solution.py:221
  582.3 47.7 %while.31 = (s32[]{:T(128)}, f32[4,512,256]{1,2,0:T(8,128)S(1)}, bf16[4,1024,256]{1,2,0:T(8,128)(2,1)}, bf16[4,1024,256]{1,2,0:T(8,128)(2,1)}, bf16[4,1024,256]{...) while((s32[]{:T(128)}, f32[4,512,256]{1,2,0:T(8,128)S(1)}, ...), condition=%wide.region_12.13_spmd.clone, body=%wide.region_10.12_spmd.sunk.clone | while | flops 1361704960 | bytes 73465992 | solution.py:242
  639.0 21.3 %reduce-scatter.7.cloned.1.call-done = bf16[4,512,256]{1,2,0:T(8,128)(2,1)} async-done(((bf16[4,1024,256]{1,2,0:T(8,128)(2,1)}), bf16[4,512,256]{1,2,0:T(8,128)(2,1)}) %reduce-scatter.7.cloned.1.call-update) | async-done | bytes 1048592 | tf_op jit(solution)/shard_map/reduce_scatter | solution.py:247
  665.8 28.7 %reduce-scatter.9.cloned.1.call-done = bf16[4,512,256]{1,2,0:T(8,128)(2,1)} async-done(((bf16[4,1024,256]{1,2,0:T(8,128)(2,1)}), bf16[4,512,256]{1,2,0:T(8,128)(2,1)}) %reduce-scatter.9.cloned.1.call-update) | async-done | bytes 1048592 | tf_op jit(solution)/shard_map/reduce_scatter | solution.py:250
  704.0 9.2 convolution_convert_fusion.1
  713.5 10.4 convolution_convert_fusion
  724.5 11.5 all-gather.6
  740.5 112.2 %reduce-scatter.11.cloned.1.call-done = bf16[256,3072]{1,0:T(8,128)(2,1)} async-done(((bf16[1024,3072]{1,0:T(8,128)(2,1)}), bf16[256,3072]{1,0:T(8,128)(2,1)}) %reduce-scatter.11.cloned.1.call-update) | async-done | bytes 1572880 | tf_op jit(solution)/shard_map/reduce_scatter | solution.py:297
  852.7 147.5 %reduce-scatter.15.cloned.1.call-done = bf16[256,4096]{1,0:T(8,128)(2,1)} async-done(((bf16[1024,4096]{1,0:T(8,128)(2,1)}), bf16[256,4096]{1,0:T(8,128)(2,1)}) %reduce-scatter.15.cloned.1.call-update) | async-done | bytes 2097168 | tf_op jit(solution)/shard_map/reduce_scatter | solution.py:315
  1000.1 147.5 %reduce-scatter.17.cloned.1.call-done = bf16[1024,1024]{1,0:T(8,128)(2,1)} async-done(((bf16[4096,1024]{1,0:T(8,128)(2,1)}), bf16[1024,1024]{1,0:T(8,128)(2,1)}) %reduce-scatter.17.cloned.1.call-update) | async-done | bytes 2097168 | tf_op jit(solution)/shard_map/reduce_scatter | solution.py:321
  1147.7 10.3 fusion.24
  1167.2 18.9 %all-reduce.10 = (bf16[1024]{0:T(1024)(128)(2,1)S(1)}, bf16[1024]{0:T(1024)(128)(2,1)S(1)}, bf16[3072]{0:T(1024)(128)(2,1)S(1)}, bf16[1024]{0:T(1024)(128)(2,1)S...) all-reduce(bf16[1024]{0:T(1024)(128)(2,1)S(1)} %get-tuple-element.1, ...), channel_id=4, replica_groups=mesh['rep'=4,'fsdp'=4,'seq'=2] {'fsdp'}, use_global_device_ids=true, to_apply=%region_18.19.clone | all-reduce | flops 13312 | bytes 53248
  1186.6 14.8 %all-reduce.8 = (bf16[256]{0:T(256)(128)(2,1)S(1)}, bf16[256]{0:T(256)(128)(2,1)S(1)}, bf16[768]{0:T(1024)(128)(2,1)S(1)}, bf16[256]{0:T(256)(128)(2,1)S(1)}, bf...) all-reduce(bf16[256]{0:T(256)(128)(2,1)S(1)} %dynamic-slice.1, ...), channel_id=1, replica_groups=mesh['rep'=4,'fsdp'=4,'seq'=2] {'rep','seq'}, use_global_device_ids=true, to_apply=%region_19.20 | all-reduce | flops 3328 | bytes 13312 | tf_op jit(solution)/shard_map/psum | solution.py:329
  1210.2 46.2 %all-reduce.13.cloned.1.call-done = (bf16[256,3072]{1,0:T(8,128)(2,1)}, bf16[256,1024]{1,0:T(8,128)(2,1)}, bf16[256,4096]{1,0:T(8,128)(2,1)}, bf16[1024,1024]{1,0:T(8,128)(2,1)}) async-done(((bf16[256,3072]{1,0:T(8,128)(2,1)}, bf16[256,1024]{1,0:T(8,128)(2,1)}, bf16[256,4096]{1,0:T(8,128)(2,1)}, bf16[1024,1024]{1,0:T(8,128)(2,1)}), (bf16[256,3072]{1,0:T(8,128)(2,1)}, bf16[256,1024]{1,0:T(8,128)(2,1)}, ...) | async-done | bytes 6291472 | tf_op jit(solution)/shard_map/psum | solution.py:331
  (332 shorter events, 223.1 us)
Async XLA Ops:
  7.2 120.6 %all-gather.14.cloned.1.call-start = ((), (), s32[]{:S(2)}) async-start(), calls=%async_computation.6 | async-start | bytes 7864320 | tf_op jit(solution)/shard_map/all_gather | solution.py:133
  7.9 190.9 %all-gather.16.cloned.1.call-start = ((), (), s32[]{:S(2)}) async-start(), calls=%async_computation.7 | async-start | bytes 3145728 | tf_op jit(solution)/shard_map/all_gather | solution.py:183
  36.6 91.2 %copy-start.46 = (f32[4,1,256]{2,1,0:T(1,128)}, f32[4,1,256]{2,1,0:T(1,128)S(1)}, u32[]{:S(2)}) copy-start(f32[4,1,256]{2,1,0:T(1,128)S(1)} %convert_element_type.251) | copy-start | bytes 12292
  45.3 82.5 %copy-start.27 = (f32[4,1,256]{2,1,0:T(1,128)}, f32[4,1,256]{2,1,0:T(1,128)S(1)}, u32[]{:S(2)}) copy-start(f32[4,1,256]{2,1,0:T(1,128)S(1)} %convert_element_type.250) | copy-start | bytes 12292
  46.7 81.0 %copy-start.29 = (f32[512]{0:T(512)}, f32[512]{0:T(512)S(1)}, u32[]{:S(2)}) copy-start(f32[512]{0:T(512)S(1)} %broadcast_multiply_fusion.1) | copy-start | bytes 6148
  49.0 78.8 %copy-start.35 = (f32[512]{0:T(512)}, f32[512]{0:T(512)S(1)}, u32[]{:S(2)}) copy-start(f32[512]{0:T(512)S(1)} %fusion.32) | copy-start | bytes 6148
  138.0 66.7 %all-gather.18.cloned.1.call-start = ((), (), s32[]{:S(2)}) async-start(), calls=%async_computation.8 | async-start | bytes 3145728 | tf_op jit(solution)/shard_map/all_gather | solution.py:182
  157.5 94.3 %all-gather.20.cloned.1.call-start = ((), (), s32[]{:S(2)}) async-start(), calls=%async_computation.9 | async-start | bytes 2621440 | tf_op jit(solution)/shard_map/all_gather | solution.py:135
  158.1 243.6 %all-gather.22.cloned.1.call-start = ((), (), s32[]{:S(2)}) async-start(), calls=%async_computation.10 | async-start | bytes 10485760 | tf_op jit(solution)/shard_map/all_gather | solution.py:139
  158.7 392.3 %all-gather.24.cloned.1.call-start = ((), (), s32[]{:S(2)}) async-start(), calls=%async_computation.11 | async-start | bytes 10485760 | tf_op jit(solution)/shard_map/all_gather | solution.py:141
  159.3 501.0 %reduce-scatter.7.cloned.1.call-start = ((), (), s32[]{:S(2)}) async-start(), calls=%async_computation.12 | async-start | bytes 3145728 | tf_op jit(solution)/shard_map/reduce_scatter | solution.py:247
  187.7 214.0 %copy-start.48 = (f32[4,1,256]{2,1,0:T(1,128)}, f32[4,1,256]{2,1,0:T(1,128)S(1)}, u32[]{:S(2)}) copy-start(f32[4,1,256]{2,1,0:T(1,128)S(1)} %convert_element_type.255) | copy-start | bytes 12292
  196.8 377.6 %copy-start.39 = (f32[4,1,256]{2,1,0:T(1,128)}, f32[4,1,256]{2,1,0:T(1,128)S(1)}, u32[]{:S(2)}) copy-start(f32[4,1,256]{2,1,0:T(1,128)S(1)} %convert_element_type.254) | copy-start | bytes 12292
  204.7 47.1 %copy-start = (bf16[1,512,1024]{2,1,0:T(8,128)(2,1)S(1)}, bf16[1,512,1024]{2,1,0:T(8,128)(2,1)}, u32[]{:S(2)}) copy-start(bf16[1,512,1024]{2,1,0:T(8,128)(2,1)} %param.19) | copy-start | bytes 3145732
  255.1 319.3 %copy-start.4 = (f32[512,1024]{1,0:T(8,128)}, f32[512,1024]{1,0:T(8,128)S(1)}, u32[]{:S(2)}) copy-start(f32[512,1024]{1,0:T(8,128)S(1)} %get-tuple-element.210) | copy-start | bytes 6291460
  255.1 319.3 %copy-start.37 = (f32[512]{0:T(512)}, f32[512]{0:T(512)S(1)}, u32[]{:S(2)}) copy-start(f32[512]{0:T(512)S(1)} %broadcast_multiply_fusion) | copy-start | bytes 6148
  255.5 319.0 %copy-start.42 = (f32[512]{0:T(512)}, f32[512]{0:T(512)S(1)}, u32[]{:S(2)}) copy-start(f32[512]{0:T(512)S(1)} %fusion.33) | copy-start | bytes 6148
  401.7 149.3 %copy-start.7 = (bf16[1,512,1024]{2,1,0:T(8,128)(2,1)S(1)}, bf16[1,512,1024]{2,1,0:T(8,128)(2,1)}, u32[]{:S(2)}) copy-start(bf16[1,512,1024]{2,1,0:T(8,128)(2,1)} %param.33) | copy-start | bytes 3145732
  630.1 64.4 %reduce-scatter.9.cloned.1.call-start = ((), (), s32[]{:S(2)}) async-start(), calls=%async_computation.13 | async-start | bytes 3145728 | tf_op jit(solution)/shard_map/reduce_scatter | solution.py:250
  630.8 109.7 %reduce-scatter.13.cloned.1.call-start = ((), (), s32[]{:S(2)}) async-start(), calls=%async_computation.15 | async-start | bytes 2621440 | tf_op jit(solution)/shard_map/reduce_scatter | solution.py:303
  635.9 216.8 %reduce-scatter.11.cloned.1.call-start = ((), (), s32[]{:S(2)}) async-start(), calls=%async_computation.14 | async-start | bytes 7864320 | tf_op jit(solution)/shard_map/reduce_scatter | solution.py:297
  702.3 297.9 %reduce-scatter.15.cloned.1.call-start = ((), (), s32[]{:S(2)}) async-start(), calls=%async_computation.16 | async-start | bytes 10485760 | tf_op jit(solution)/shard_map/reduce_scatter | solution.py:315
  713.2 434.4 %reduce-scatter.17.cloned.1.call-start = ((), (), s32[]{:S(2)}) async-start(), calls=%async_computation.17 | async-start | bytes 10485760 | tf_op jit(solution)/shard_map/reduce_scatter | solution.py:321
  723.9 532.5 %all-reduce.13.cloned.1.call-start = ((), (), s32[]{:S(2)}) async-start(), calls=%async_computation.18 | async-start | bytes 12582912 | tf_op jit(solution)/shard_map/psum | solution.py:331
  (48 other events, 586.4 us)
Sparse Core Ops, SparseCore 0:
  9.6 118.1 all-gather.13
  138.1 31.2 all-gather.15
  171.6 33.0 all-gather.17
  206.1 45.6 all-gather.19
  253.2 148.4 all-gather.21
  403.1 147.7 all-gather.23
  630.2 30.0 reduce-scatter.6
  662.5 31.8 reduce-scatter.8
  696.8 43.6 reduce-scatter.12
  742.6 109.9 reduce-scatter.10
  855.0 145.0 reduce-scatter.14
  1002.3 145.2 reduce-scatter.16
  1151.2 105.1 all-reduce.12
where the time goes:
time: 1280 us; the launch traced here: 1270 us
  waiting for transfers between devices  875 us (68%)
  matrix products  154 us (12%)
  blocking collectives  118 us (9%)
  local copies, waits for them, and re-layouts  64 us (5%)
  other arithmetic  43.8 us (3%)
  between operations  17.1 us (1%)
    reduce_scatter x1, waiting for transfers between devices, local(): lax.psum_scatter(terms[8].astype(jnp.bfloat16), 'fsdp', scatter_dimension...  147 us
    reduce_scatter x1, waiting for transfers between devices, local(): lax.psum_scatter(terms[10].astype(jnp.bfloat16), 'fsdp', scatter_dimensio...  147 us
    all_gather x1, waiting for transfers between devices, local(): lax.all_gather(shards[8], 'fsdp', axis=0, tiled=True)  146 us
    all_gather x1, waiting for transfers between devices, local(): lax.all_gather(shards[10], 'fsdp', axis=0, tiled=True)  122 us
    reduce_scatter x1, waiting for transfers between devices, local(): lax.psum_scatter(terms[2].astype(jnp.bfloat16), 'fsdp', scatter_dimension...  112 us
    all_gather x1, waiting for transfers between devices, local(): lax.all_gather(shards[2], 'fsdp', axis=0, tiled=True)  78.8 us
    psum x1, waiting for transfers between devices, local(): lax.psum(owned[2].astype(jnp.bfloat16), ('rep', 'seq')).astype(jnp.float32)  46.2 us
    reduce_scatter x1, waiting for transfers between devices, local(): lax.psum_scatter(value_grad.astype(jnp.bfloat16), 'seq', scatter_dimensio...  28.7 us
  transfers between devices with their start and end apart: 13, of which 12 were waited for; matrix products, arithmetic and copies ran while one was open for 12% of the time, Pallas kernels for 0%

commit v1 on v0

--- a/solution.py
+++ b/solution.py
@@ -136,7 +136,9 @@
         lax.all_gather(shards[5], "fsdp", axis=0, tiled=True),
         lax.all_gather(shards[6], "fsdp", axis=0, tiled=True),
         lax.all_gather(shards[7], "fsdp", axis=0, tiled=True),
-        lax.all_gather(shards[8], "fsdp", axis=0, tiled=True),
+        jnp.concatenate(
+            lax.all_to_all(jnp.stack([shards[8]] * lax.axis_size("fsdp")), "fsdp", 0, 0), axis=0
+        ),
         lax.all_gather(shards[9], "fsdp", axis=0, tiled=True),
         lax.all_gather(shards[10], "fsdp", axis=0, tiled=True),
         lax.all_gather(shards[11], "fsdp", axis=0, tiled=True),

time: 1280 us -> 1390 us (1.086)
  blocking collectives: 118 us -> 386 us
  waiting for transfers between devices: 875 us -> 700 us
    all_gather x1, blocking collectives: 7.97 us -> 174 us  [local(): lax.all_gather(shards[5], 'fsdp', axis=0, tiled=True)]
    all_gather x1, waiting for transfers between devices: 122 us -> 0.01 us  [local(): lax.all_gather(shards[10], 'fsdp', axis=0, tiled=True)]
    all_gather x1, blocking collectives: 11.9 us -> 111 us  [local(): lax.all_gather(shards[9], 'fsdp', axis=0, tiled=True)]
    all_gather x1, waiting for transfers between devices: 146 us -> 115 us  [local(): lax.all_gather(shards[8], 'fsdp', axis=0, tiled=True)]
    all_gather x1, waiting for transfers between devices: 15.6 us -> 0.02 us  [local(): lax.all_gather(shards[4], 'fsdp', axis=0, tiled=True)]
  transfers between devices with their start and end apart: 13 -> 14, of which waited for: 12 -> 9; matrix products, arithmetic and copies ran while one was open for 12% -> 13% of each run, Pallas kernels for 0% -> 0%
where the time goes in v1:
time: 1390 us; the launch traced here: 1380 us
  waiting for transfers between devices  700 us (50%)
  blocking collectives  386 us (28%)
  matrix products  156 us (11%)
  local copies, waits for them, and re-layouts  71.1 us (5%)
  other arithmetic  43.8 us (3%)
  between operations  17.1 us (1%)
    all_gather x1, blocking collectives, local(): lax.all_gather(shards[5], 'fsdp', axis=0, tiled=True)  174 us
    reduce_scatter x1, waiting for transfers between devices, local(): lax.psum_scatter(terms[8].astype(jnp.bfloat16), 'fsdp', scatter_dimension...  148 us
    reduce_scatter x1, waiting for transfers between devices, local(): lax.psum_scatter(terms[10].astype(jnp.bfloat16), 'fsdp', scatter_dimensio...  147 us
    all_gather x1, waiting for transfers between devices, local(): lax.all_gather(shards[8], 'fsdp', axis=0, tiled=True)  115 us
    reduce_scatter x1, waiting for transfers between devices, local(): lax.psum_scatter(terms[2].astype(jnp.bfloat16), 'fsdp', scatter_dimension...  112 us
    all_gather x1, blocking collectives, local(): lax.all_gather(shards[9], 'fsdp', axis=0, tiled=True)  111 us
    all_gather x1, waiting for transfers between devices, local(): lax.all_gather(shards[2], 'fsdp', axis=0, tiled=True)  78.8 us
    psum x1, waiting for transfers between devices, local(): lax.psum(owned[2].astype(jnp.bfloat16), ('rep', 'seq')).astype(jnp.float32)  46.2 us
  transfers between devices with their start and end apart: 14, of which 9 were waited for; matrix products, arithmetic and copies ran while one was open for 13% of the time, Pallas kernels for 0%

profile of v1, /device:TPU:0, one launch (start us, length us, event | category | flops | bytes accessed | tf_op | source)
XLA Modules:
  0.0 1381.7 jit_solution(17116113935965499209)
XLA Ops:
  8.6 14.8 %all-gather.2 = bf16[4,1,768]{2,1,0:T(2,128)(2,1)S(1)} all-gather(bf16[1,1,768]{2,1,0:T(2,128)(2,1)S(1)} %reshape.250), channel_id=1, replica_groups=mesh['rep'=4,'fsdp'=4,'seq'=2] {'fsdp'}, dimensions={0}, use_global_device_ids=true | all-gather | bytes 7680 | tf_op jit(solution)/shard_map/all_gather | solution.py:134
  24.2 12.4 all-gather.1
  49.0 78.8 %all-gather.14.cloned.1.call-done = bf16[1024,3072]{1,0:T(8,128)(2,1)} async-done(((bf16[256,3072]{1,0:T(8,128)(2,1)}), bf16[1024,3072]{1,0:T(8,128)(2,1)}) %all-gather.14.cloned.1.call-update) | async-done | bytes 6291472 | tf_op jit(solution)/shard_map/all_gather | solution.py:133
  171.1 174.3 %all-gather.3 = bf16[4,1,256]{2,1,0:T(2,128)(2,1)S(1)} all-gather(bf16[1,1,256]{2,1,0:T(2,128)(2,1)S(1)} %reshape.252), channel_id=1, replica_groups=mesh['rep'=4,'fsdp'=4,'seq'=2] {'fsdp'}, dimensions={0}, use_global_device_ids=true | all-gather | bytes 2560 | tf_op jit(solution)/shard_map/all_gather | solution.py:136
  345.4 111.5 %all_gather.57 = bf16[4096]{0:T(1024)(128)(2,1)S(1)} all-gather(bf16[1024]{0:T(1024)(128)(2,1)S(1)} %copy-done.50), channel_id=1, replica_groups=mesh['rep'=4,'fsdp'=4,'seq'=2] {'fsdp'}, dimensions={0}, use_global_device_ids=true | all-gather | bytes 10240 | tf_op jit(solution)/shard_map/all_gather | solution.py:142
  456.9 9.4 all-gather.5
  466.3 10.6 all-gather.4
  479.0 31.4 %while.30 = (s32[]{:T(128)}, bf16[4,512,256]{1,2,0:T(8,128)(2,1)S(1)}, f32[4,4,512,1]{2,1,3,0:T(4,128)S(1)}, f32[4,4,512,1]{2,1,3,0:T(4,128)S(1)}, bf16[4,1024,2...) while((s32[]{:T(128)}, ...), condition=%wide.region_5.6_spmd.clone, body=%wide.region_2.5_spmd.sunk.clone | while | flops 555741184 | bytes 29958248 | solution.py:187
  515.4 27.9 %multiply_convert_fusion.1 = (bf16[512,4096]{1,0:T(8,128)(2,1)}, f32[512,4096]{1,0:T(8,128)}, f32[512,4096]{1,0:T(8,128)}) fusion(f32[4096]{0:T(1024)S(1)} %convert_element_type.220, bf16[1024,4096]{1,0:T(8,128)(2,1)} %bitcast.41, f32[512,1024]{1,0:T(8,128)S(1)} %get-tuple-element.210, f32[1024]{0:T(1024)S(1)} %bitcast.296, f32[1024]{0:T(1024)S(1)} %bitcast.289, ...), kind=kOutput, calls=%fused_computation.31 | convolution fusion | flops 4436000768 | bytes 31485952 | tf_op jit(solution)/shard_map/dot_general | solution.py:196
  543.3 15.8 %fusion.47 = (bf16[4096]{0:T(1024)(128)(2,1)}, bf16[512,4096]{1,0:T(8,128)(2,1)}) fusion(f32[512,4096]{1,0:T(8,128)} %get-tuple-element.179, bf16[4096,1024]{1,0:T(8,128)(2,1)} %all-gather.22.cloned.1.call-done, bf16[1,512,1024]{2,1,0:T(8,128)(2,1)S(1)} %copy-done.7, f32[512,4096]{1,0:T(8,128)} %get-tuple-element.211, f32[4096]{0:T(1024)S(1)} %convert_element_type.220), kind=kOutput, calls=%fused_computation.125 | convolution fusion | flops 4328517632 | bytes 30433280 | tf_op jit(solution)/shard_map/td,fd->tf/dot_general | solution.py:223
  559.1 114.5 %all-gather.24.cloned.1.call-done = bf16[1024,4096]{1,0:T(8,128)(2,1)} async-done(((bf16[256,4096]{1,0:T(8,128)(2,1)}), bf16[1024,4096]{1,0:T(8,128)(2,1)}) %all-gather.24.cloned.1.call-update) | async-done | bytes 8388624 | tf_op jit(solution)/shard_map/all_gather | solution.py:214
  673.6 9.3 multiply_reduce_fusion.2
  690.8 47.8 %while.31 = (s32[]{:T(128)}, f32[4,512,256]{1,2,0:T(8,128)S(1)}, bf16[4,1024,256]{1,2,0:T(8,128)(2,1)}, bf16[4,1024,256]{1,2,0:T(8,128)(2,1)}, bf16[4,1024,256]{...) while((s32[]{:T(128)}, f32[4,512,256]{1,2,0:T(8,128)S(1)}, ...), condition=%wide.region_12.13_spmd.clone, body=%wide.region_10.12_spmd.sunk.clone | while | flops 1361704960 | bytes 73465992 | solution.py:244
  747.6 21.4 %reduce-scatter.7.cloned.1.call-done = bf16[4,512,256]{1,2,0:T(8,128)(2,1)} async-done(((bf16[4,1024,256]{1,2,0:T(8,128)(2,1)}), bf16[4,512,256]{1,2,0:T(8,128)(2,1)}) %reduce-scatter.7.cloned.1.call-update) | async-done | bytes 1048592 | tf_op jit(solution)/shard_map/reduce_scatter | solution.py:249
  774.4 28.7 %reduce-scatter.9.cloned.1.call-done = bf16[4,512,256]{1,2,0:T(8,128)(2,1)} async-done(((bf16[4,1024,256]{1,2,0:T(8,128)(2,1)}), bf16[4,512,256]{1,2,0:T(8,128)(2,1)}) %reduce-scatter.9.cloned.1.call-update) | async-done | bytes 1048592 | tf_op jit(solution)/shard_map/reduce_scatter | solution.py:252
  822.2 10.4 convolution_convert_fusion
  833.2 11.5 all-gather.6
  849.1 112.2 %reduce-scatter.11.cloned.1.call-done = bf16[256,3072]{1,0:T(8,128)(2,1)} async-done(((bf16[1024,3072]{1,0:T(8,128)(2,1)}), bf16[256,3072]{1,0:T(8,128)(2,1)}) %reduce-scatter.11.cloned.1.call-update) | async-done | bytes 1572880 | tf_op jit(solution)/shard_map/reduce_scatter | solution.py:299
  961.3 147.5 %reduce-scatter.15.cloned.1.call-done = bf16[256,4096]{1,0:T(8,128)(2,1)} async-done(((bf16[1024,4096]{1,0:T(8,128)(2,1)}), bf16[256,4096]{1,0:T(8,128)(2,1)}) %reduce-scatter.15.cloned.1.call-update) | async-done | bytes 2097168 | tf_op jit(solution)/shard_map/reduce_scatter | solution.py:317
  1108.8 147.5 %reduce-scatter.17.cloned.1.call-done = bf16[1024,1024]{1,0:T(8,128)(2,1)} async-done(((bf16[4096,1024]{1,0:T(8,128)(2,1)}), bf16[1024,1024]{1,0:T(8,128)(2,1)}) %reduce-scatter.17.cloned.1.call-update) | async-done | bytes 2097168 | tf_op jit(solution)/shard_map/reduce_scatter | solution.py:323
  1256.4 10.3 fusion.24
  1275.8 18.9 %all-reduce.10 = (bf16[1024]{0:T(1024)(128)(2,1)S(1)}, bf16[1024]{0:T(1024)(128)(2,1)S(1)}, bf16[3072]{0:T(1024)(128)(2,1)S(1)}, bf16[1024]{0:T(1024)(128)(2,1)S...) all-reduce(bf16[1024]{0:T(1024)(128)(2,1)S(1)} %get-tuple-element.1, ...), channel_id=4, replica_groups=mesh['rep'=4,'fsdp'=4,'seq'=2] {'fsdp'}, use_global_device_ids=true, to_apply=%region_18.19.clone | all-reduce | flops 13312 | bytes 53248
  1295.3 14.9 %all-reduce.8 = (bf16[256]{0:T(256)(128)(2,1)S(1)}, bf16[256]{0:T(256)(128)(2,1)S(1)}, bf16[768]{0:T(1024)(128)(2,1)S(1)}, bf16[256]{0:T(256)(128)(2,1)S(1)}, bf...) all-reduce(bf16[256]{0:T(256)(128)(2,1)S(1)} %dynamic-slice.1, ...), channel_id=1, replica_groups=mesh['rep'=4,'fsdp'=4,'seq'=2] {'rep','seq'}, use_global_device_ids=true, to_apply=%region_19.20 | all-reduce | flops 3328 | bytes 13312 | tf_op jit(solution)/shard_map/psum | solution.py:331
  1318.9 46.2 %all-reduce.13.cloned.1.call-done = (bf16[256,3072]{1,0:T(8,128)(2,1)}, bf16[256,1024]{1,0:T(8,128)(2,1)}, bf16[256,4096]{1,0:T(8,128)(2,1)}, bf16[1024,1024]{1,0:T(8,128)(2,1)}) async-done(((bf16[256,3072]{1,0:T(8,128)(2,1)}, bf16[256,1024]{1,0:T(8,128)(2,1)}, bf16[256,4096]{1,0:T(8,128)(2,1)}, bf16[1024,1024]{1,0:T(8,128)(2,1)}), (bf16[256,3072]{1,0:T(8,128)(2,1)}, bf16[256,1024]{1,0:T(8,128)(2,1)}, ...) | async-done | bytes 6291472 | tf_op jit(solution)/shard_map/psum | solution.py:333
  (333 shorter events, 215.5 us)
Async XLA Ops:
  7.2 120.6 %all-gather.14.cloned.1.call-start = ((), (), s32[]{:S(2)}) async-start(), calls=%async_computation.7 | async-start | bytes 7864320 | tf_op jit(solution)/shard_map/all_gather | solution.py:133
  7.9 471.0 %all-gather.16.cloned.1.call-start = ((), (), s32[]{:S(2)}) async-start(), calls=%async_computation.8 | async-start | bytes 3145728 | tf_op jit(solution)/shard_map/all_gather | solution.py:185
  36.6 91.2 %copy-start.46 = (f32[4,1,256]{2,1,0:T(1,128)}, f32[4,1,256]{2,1,0:T(1,128)S(1)}, u32[]{:S(2)}) copy-start(f32[4,1,256]{2,1,0:T(1,128)S(1)} %convert_element_type.251) | copy-start | bytes 12292
  45.3 82.5 %copy-start.27 = (f32[4,1,256]{2,1,0:T(1,128)}, f32[4,1,256]{2,1,0:T(1,128)S(1)}, u32[]{:S(2)}) copy-start(f32[4,1,256]{2,1,0:T(1,128)S(1)} %convert_element_type.250) | copy-start | bytes 12292
  46.7 81.0 %copy-start.29 = (f32[512]{0:T(512)}, f32[512]{0:T(512)S(1)}, u32[]{:S(2)}) copy-start(f32[512]{0:T(512)S(1)} %broadcast_multiply_fusion.1) | copy-start | bytes 6148
  138.0 340.9 %all-gather.18.cloned.1.call-start = ((), (), s32[]{:S(2)}) async-start(), calls=%async_computation.9 | async-start | bytes 3145728 | tf_op jit(solution)/shard_map/all_gather | solution.py:184
  157.5 353.0 %all-gather.20.cloned.1.call-start = ((), (), s32[]{:S(2)}) async-start(), calls=%async_computation.10 | async-start | bytes 2621440 | tf_op jit(solution)/shard_map/all_gather | solution.py:135
  158.0 385.3 %all-gather.22.cloned.1.call-start = ((), (), s32[]{:S(2)}) async-start(), calls=%async_computation.11 | async-start | bytes 10485760 | tf_op jit(solution)/shard_map/all_gather | solution.py:143
  164.5 180.9 %copy-start.50 = (bf16[1024]{0:T(1024)(128)(2,1)S(1)}, bf16[1024]{0:T(1024)(128)(2,1)}, u32[]{:S(2)}) copy-start(bf16[1024]{0:T(1024)(128)(2,1)} %param.30) | copy-start | bytes 6148
  164.5 292.3 %copy-start.54 = (bf16[256]{0:T(256)(128)(2,1)S(1)}, bf16[256]{0:T(256)(128)(2,1)}, u32[]{:S(2)}) copy-start(bf16[256]{0:T(256)(128)(2,1)} %param.28) | copy-start | bytes 1540
  164.5 301.8 %copy-start.55 = (bf16[256]{0:T(256)(128)(2,1)S(1)}, bf16[256]{0:T(256)(128)(2,1)}, u32[]{:S(2)}) copy-start(bf16[256]{0:T(256)(128)(2,1)} %param.27) | copy-start | bytes 1540
  164.5 350.9 %all-to-all-start = ((bf16[4,256,4096]{2,1,0:T(8,128)(2,1)}), bf16[4,256,4096]{2,1,0:T(8,128)(2,1)}, u32[]{:S(2)}, u32[]{:S(2)}) async-start(bf16[4,256,4096]{2,1,0:T(8,128)(2,1)} %stack.16), calls=%async_computation | async-start | bytes 16777216 | tf_op jit(solution)/shard_map/all_to_all | solution.py:140
  170.3 503.3 %all-gather.24.cloned.1.call-start = ((), (), s32[]{:S(2)}) async-start(), calls=%async_computation.12 | async-start | bytes 10485760 | tf_op jit(solution)/shard_map/all_gather | solution.py:214
  170.9 598.0 %reduce-scatter.7.cloned.1.call-start = ((), (), s32[]{:S(2)}) async-start(), calls=%async_computation.13 | async-start | bytes 3145728 | tf_op jit(solution)/shard_map/reduce_scatter | solution.py:249
  477.0 206.0 %copy-start.39 = (f32[4,1,256]{2,1,0:T(1,128)}, f32[4,1,256]{2,1,0:T(1,128)S(1)}, u32[]{:S(2)}) copy-start(f32[4,1,256]{2,1,0:T(1,128)S(1)} %convert_element_type.254) | copy-start | bytes 12292
  515.0 167.9 %copy-start.4 = (f32[512,1024]{1,0:T(8,128)}, f32[512,1024]{1,0:T(8,128)S(1)}, u32[]{:S(2)}) copy-start(f32[512,1024]{1,0:T(8,128)S(1)} %get-tuple-element.210) | copy-start | bytes 6291460
  515.0 167.9 %copy-start.37 = (f32[512]{0:T(512)}, f32[512]{0:T(512)S(1)}, u32[]{:S(2)}) copy-start(f32[512]{0:T(512)S(1)} %broadcast_multiply_fusion) | copy-start | bytes 6148
  515.4 167.6 %copy-start.42 = (f32[512]{0:T(512)}, f32[512]{0:T(512)S(1)}, u32[]{:S(2)}) copy-start(f32[512]{0:T(512)S(1)} %fusion.33) | copy-start | bytes 6148
  738.7 64.4 %reduce-scatter.9.cloned.1.call-start = ((), (), s32[]{:S(2)}) async-start(), calls=%async_computation.14 | async-start | bytes 3145728 | tf_op jit(solution)/shard_map/reduce_scatter | solution.py:252
  739.4 109.7 %reduce-scatter.13.cloned.1.call-start = ((), (), s32[]{:S(2)}) async-start(), calls=%async_computation.16 | async-start | bytes 2621440 | tf_op jit(solution)/shard_map/reduce_scatter | solution.py:305
  744.5 216.8 %reduce-scatter.11.cloned.1.call-start = ((), (), s32[]{:S(2)}) async-start(), calls=%async_computation.15 | async-start | bytes 7864320 | tf_op jit(solution)/shard_map/reduce_scatter | solution.py:299
  811.0 297.9 %reduce-scatter.15.cloned.1.call-start = ((), (), s32[]{:S(2)}) async-start(), calls=%async_computation.17 | async-start | bytes 10485760 | tf_op jit(solution)/shard_map/reduce_scatter | solution.py:317
  821.9 434.4 %reduce-scatter.17.cloned.1.call-start = ((), (), s32[]{:S(2)}) async-start(), calls=%async_computation.18 | async-start | bytes 10485760 | tf_op jit(solution)/shard_map/reduce_scatter | solution.py:323
  832.6 532.5 %all-reduce.13.cloned.1.call-start = ((), (), s32[]{:S(2)}) async-start(), calls=%async_computation.19 | async-start | bytes 12582912 | tf_op jit(solution)/shard_map/psum | solution.py:333
  (48 other events, 666.4 us)
Sparse Core Ops, SparseCore 0:
  9.6 118.1 all-gather.13
  138.1 31.2 all-gather.15
  171.6 33.0 all-gather.17
  206.1 75.7 all-gather.19
  283.4 240.1 all-gather.21
  525.0 148.6 all-gather.23
  738.8 30.0 reduce-scatter.6
  771.2 31.8 reduce-scatter.8
  805.4 43.6 reduce-scatter.12
  851.3 109.9 reduce-scatter.10
  963.7 145.1 reduce-scatter.14
  1111.0 145.2 reduce-scatter.16
  1259.9 105.1 all-reduce.12
